TPU v7x, 128 devices: a whole 4x4x4 slice. The times are simulated.
128 devices in a mesh: src: 4 (over z), vol: 32 (over y, x, core).
Axes of the slice: x: 4, y: 4, z: 4, core: 2. Of those that a mesh axis runs over, the one named last changes fastest.
Arguments:
- forward: bfloat16 [16384, 36, 512], P(('src', 'vol')), may hold values from -6 to 6
- item_tx: int32 [16384], P(('src', 'vol')), may hold values from 0 to 15, as said below
- item_brick: int32 [16384], P(('src', 'vol')), may hold values from 0 to 1023
- tx_place: int32 [16], replicated, may hold values from 0 to 15, as said below
- brick_place: int32 [1024], replicated, may hold values from 0 to 1023, as said below
- adjoint: bfloat16 [16, 1024, 36, 512], P('src', 'vol'), may hold values from -6 to 6
Outputs:
- gradient: float32 [2, 256, 16, 128], P(None, 'vol')
Inputs may be any that keep to these rules, and one draw needn't show every extreme that they name: Stored brick i goes to owner (tx_place[item_tx[i]] // 4, brick_place[item_brick[i]] // 32) as (src index, vol index). Among the stored bricks of one device at most 2 share an owner; in every draw one owner receives exactly 2 from every device. `tx_place`: A permutation. `brick_place`: A permutation.
All inputs are finite; a program needn't handle non-finite values.
Results may differ from a plain program's by a relative error of at most 0.0003.
Values may be sent and summed in bfloat16 or wider, within the bound.
No kernel may reach another device: no remote copies, remote signals or barrier semaphores. Data moves between devices by JAX's collectives and lax.ppermute only.
A program may use at most 128 MiB of HBM per device.

v0:
```python
import math
import jax
import jax.numpy as jnp
from jax import lax
from jax.sharding import PartitionSpec as P

E = 8
NFREQ = 6
NBY = 2
NBZ = 16


def with_halo(cells, sides, width):
    for axis, dim in sides:
        count = lax.axis_size(axis)
        ends = count - 1
        head = lax.slice_in_dim(cells, 0, width, axis=dim)
        tail = lax.slice_in_dim(cells, cells.shape[dim] - width, cells.shape[dim], axis=dim)
        cells = jnp.concatenate(
            [
                lax.ppermute(tail, axis, [(i, (i + 1) % count) for i in range(ends)]),
                cells,
                lax.ppermute(head, axis, [((i + 1) % count, i) for i in range(ends)]),
            ],
            axis=dim,
        )
    return cells


def tap_weights():
    raw_taps = [math.exp(-(offset - 4) * (offset - 4) / 4.5) for offset in range(9)]
    tap_total = sum(raw_taps)
    return [tap_value / tap_total for tap_value in raw_taps]


def correlate(fwd_field, adj_field):
    lead_shape = fwd_field.shape[:-2]
    fwd_split = fwd_field.reshape(lead_shape + (NFREQ, 3, 2, fwd_field.shape[-1]))
    adj_split = adj_field.reshape(lead_shape + (NFREQ, 3, 2, adj_field.shape[-1]))
    products = (
        fwd_split[..., 0, :] * adj_split[..., 0, :] - fwd_split[..., 1, :] * adj_split[..., 1, :]
    )
    horizontal = jnp.sum(products[..., 0:2, :], axis=(-3, -2))
    vertical = jnp.sum(products[..., 2, :], axis=-2)
    return jnp.stack([horizontal, vertical], axis=-2)


def smooth_axis(padded, axis):
    weights = tap_weights()
    length = padded.shape[axis] - 8
    summed = jnp.zeros(padded.shape[:axis] + (length,) + padded.shape[axis + 1 :], jnp.float32)
    for offset in range(9):
        summed = summed + weights[offset] * lax.slice_in_dim(
            padded, offset, offset + length, axis=axis
        )
    return summed


def pad_axis(field, axis):
    widths = [(0, 0)] * field.ndim
    widths[axis] = (4, 4)
    return jnp.pad(field, widths)


def lookup(indices, table):
    hits = indices[:, None] == jnp.arange(table.shape[0], dtype=jnp.int32)[None, :]
    return jnp.sum(jnp.where(hits, table[None, :], 0), axis=1)


def local(forward, item_tx, item_brick, tx_place, brick_place, adjoint):
    stored = forward.shape[0]
    channels = forward.shape[1]
    cells = forward.shape[2]
    src_count = lax.axis_size("src")
    vol_count = lax.axis_size("vol")
    devices = src_count * vol_count
    local_tx = adjoint.shape[0]
    local_bricks = adjoint.shape[1]
    capacity = max(2, 2 * stored // devices)
    slot_total = devices * capacity
    tx_at = lookup(item_tx, tx_place)
    brick_at = lookup(item_brick, brick_place)
    destination = tx_at // local_tx * vol_count + brick_at // local_bricks
    pair_index = tx_at % local_tx * local_bricks + brick_at % local_bricks
    positions = jnp.arange(stored, dtype=jnp.int32)
    same_owner = destination[:, None] == destination[None, :]
    earlier = positions[:, None] > positions[None, :]
    order_rank = jnp.sum((same_owner & earlier).astype(jnp.int32), axis=1)
    slot_index = destination * capacity + order_rank
    outgoing = jnp.zeros((slot_total, channels, cells), forward.dtype).at[slot_index].set(forward)
    slot_pairs = jnp.full((slot_total,), -1, jnp.int32).at[slot_index].set(pair_index)
    arrived, arrived_pairs = (
        lax.all_to_all(outgoing, ("src", "vol"), split_axis=0, concat_axis=0, tiled=True),
        lax.all_to_all(slot_pairs, ("src", "vol"), split_axis=0, concat_axis=0, tiled=True),
    )
    filled = arrived_pairs >= 0
    flat_adjoint = adjoint.reshape(local_tx * local_bricks, channels, cells)
    picked = flat_adjoint[jnp.maximum(arrived_pairs, 0)]
    product = correlate(arrived.astype(jnp.float32), picked.astype(jnp.float32))
    owner_brick = arrived_pairs % local_bricks
    owner_table = (
        (owner_brick[None, :] == jnp.arange(local_bricks, dtype=jnp.int32)[:, None])
        & filled[None, :]
    ).astype(jnp.float32)
    gradient = jnp.dot(
        owner_table, product.reshape(slot_total, 2 * cells), precision=lax.Precision.HIGHEST
    )
    gradient = gradient.reshape(local_bricks, 2, cells)
    slab = (
        gradient.reshape(NBY, NBZ, 2, E, E, E)
        .transpose(2, 3, 0, 4, 1, 5)
        .reshape(2, E, NBY * E, NBZ * E)
    )
    summed = lax.psum(slab, "src")
    padded = with_halo(summed, (("vol", 1),), 4)
    field = smooth_axis(padded, 1)
    for axis in (2, 3):
        field = smooth_axis(pad_axis(field, axis), axis)
    return field


def solution(mesh):
    in_specs = (
        P(("src", "vol"), None, None),
        P(("src", "vol")),
        P(("src", "vol")),
        P(),
        P(),
        P("src", "vol", None, None),
    )
    out_specs = P(None, "vol", None, None)
    return jax.shard_map(local, mesh=mesh, in_specs=in_specs, out_specs=out_specs, check_vma=False)
```

profile of v0, /device:TPU:7, one launch (start us, length us, event | category | flops | bytes accessed | tf_op | source)
XLA Modules:
  0.0 298.9 jit_solution(5812231663383494735)
XLA Ops:
  6.5 0.8 select_reduce_fusion.1
  7.3 0.9 select_reduce_fusion
  8.4 1.0 scatter_custom_fusion
  9.4 0.8 all_to_all.11
  10.2 10.8 %all-to-all-start = ((s32[128,2,1]{1,2,0:T(1,128)}), s32[128,2,1]{1,2,0:T(1,128)S(1)}, u32[]{:S(2)}, u32[]{:S(2)}) async-start(s32[128,2,1]{1,2,0:T(1,128)} %bitcast.4), calls=%async_computation | async-start | bytes 131072 | tf_op jit(solution)/shard_map/all_to_all | solution.py:94
  21.0 7.3 %copy.49 = bf16[128,36,512]{2,1,0:T(8,128)(2,1)} copy(bf16[128,36,512]{2,0,1:T(8,128)(2,1)} %param.6) | data formatting | bytes 9437184 | tf_op args[0]
  28.3 4.6 %broadcast_in_dim.33 = bf16[256,36,512]{2,1,0:T(8,128)(2,1)} broadcast(bf16[]{:T(256)} %constant.76.clone.1), dimensions={} | broadcast | bytes 9437186 | tf_op jit(solution)/shard_map/broadcast_in_dim | solution.py:90
  32.8 20.5 %scatter_fusion = bf16[256,36,512]{2,1,0:T(8,128)(2,1)} fusion(bf16[256,36,512]{2,1,0:T(8,128)(2,1)} %broadcast_in_dim.33, s32[128]{0:T(128)S(1)} %fusion.52, bf16[128,36,512]{2,1,0:T(8,128)(2,1)} %copy.49), kind=kCustom, calls=%fused_computation.2 | custom fusion | bytes 14156288 | tf_op jit(solution)/shard_map/scatter | solution.py:90
  53.4 10.3 %all-to-all-start.1 = ((bf16[256,36,512]{2,1,0:T(8,128)(2,1)}), bf16[256,36,512]{2,1,0:T(8,128)(2,1)}, u32[]{:S(2)}, u32[]{:S(2)}) async-start(bf16[256,36,512]{2,1,0:T(8,128)(2,1)} %scatter_fusion), calls=%async_computation.1 | async-start | bytes 20971520 | tf_op jit(solution)/shard_map/all_to_all | solution.py:93
  63.9 2.7 copy.51
  66.6 5.1 %copy.52 = bf16[128,36,512]{2,1,0:T(8,128)(2,1)} copy(bf16[128,36,512]{2,0,1:T(8,128)(2,1)S(1)} %bitcast.58) | data formatting | bytes 9437184 | tf_op jit(solution)/shard_map/reshape | solution.py:97
  71.7 0.5 broadcast.393
  72.2 1.0 fusion.55
  73.5 12.1 %gather_fusion = bf16[256,36,512]{2,1,0:T(8,128)(2,1)} fusion(bf16[128,36,512]{2,1,0:T(8,128)(2,1)} %copy.52, s32[1024]{0:T(1024)S(1)} %pad_clamp_fusion), kind=kCustom, calls=%fused_computation | custom fusion | bytes 18875392 | tf_op jit(solution)/shard_map/gather | solution.py:98
  85.6 10.9 %copy.53 = bf16[256,36,512]{2,0,1:T(8,128)(2,1)} copy(bf16[256,36,512]{2,1,0:T(8,128)(2,1)} %gather_fusion) | data formatting | bytes 18874368 | tf_op jit(solution)/shard_map/gather | solution.py:98
  96.5 12.7 %convert.3 = f32[256,6,3,2,512]{4,0,3,2,1:T(8,128)} convert(bf16[256,6,3,2,512]{4,0,3,2,1:T(8,128)(2,1)} %bitcast.56) | non-fusion elementwise | flops 4718592 | bytes 28311552 | tf_op jit(solution)/shard_map/convert_element_type | solution.py:99
  109.2 77.3 %all-to-all-done.1 = bf16[256,36,512]{2,1,0:T(8,128)(2,1)} async-done(((bf16[256,36,512]{2,1,0:T(8,128)(2,1)}), bf16[256,36,512]{2,1,0:T(8,128)(2,1)}, u32[]{:S(2)}, u32[]{:S(2)}) %all-to-all-start.1) | async-done | bytes 9437216 | tf_op jit(solution)/shard_map/all_to_all | solution.py:93
  186.5 10.9 %copy.50 = bf16[256,36,512]{2,0,1:T(8,128)(2,1)} copy(bf16[256,36,512]{2,1,0:T(8,128)(2,1)} %all-to-all-done.1) | data formatting | bytes 18874368 | tf_op jit(solution)/shard_map/all_to_all | solution.py:93
  197.4 12.7 %convert.2 = f32[256,6,3,2,512]{4,0,3,2,1:T(8,128)} convert(bf16[256,6,3,2,512]{4,0,3,2,1:T(8,128)(2,1)} %bitcast.57) | non-fusion elementwise | flops 4718592 | bytes 28311552 | tf_op jit(solution)/shard_map/reshape | solution.py:38
  210.1 14.0 %fusion.1 = f32[256,6,3,512]{3,0,2,1:T(8,128)S(1)} fusion(f32[256,6,3,2,512]{4,0,3,2,1:T(8,128)} %convert.3, f32[256,6,3,2,512]{4,0,3,2,1:T(8,128)} %convert.2), kind=kLoop, calls=%fused_computation.5 | loop fusion | flops 7077888 | bytes 47185920 | tf_op jit(solution)/shard_map/sub | solution.py:41
  224.5 0.7 slice_reduce_fusion
  225.7 0.7 convolution_bitcast_fusion
  226.4 0.6 copy.55
  227.0 1.6 reshape.258
  228.7 46.9 %all-reduce.4.cloned.1.call-done = f32[2,8,16,128]{3,2,1,0:T(8,128)} async-done(((f32[2,8,16,128]{3,2,1,0:T(8,128)}), f32[2,8,16,128]{3,2,1,0:T(8,128)}) %all-reduce.4.cloned.1.call-update) | async-done | bytes 131088 | tf_op jit(solution)/shard_map/psum | solution.py:114
  275.6 0.9 fusion.56
  276.5 5.7 %collective-permute-start = (f32[2,4,16,128]{3,2,1,0:T(8,128)S(1)}, f32[2,4,16,128]{3,2,1,0:T(8,128)S(1)}, u32[]{:S(2)}, u32[]{:S(2)}) collective-permute-start(f32[2,4,16,128]{3,2,1,0:T(8,128)S(1)} %get-tuple-element.9), channel_id=1, source_target_pairs={{0,1},{1,2},{2,3},{3,4},{4,5},{5,6},{6,7},{7,8},{8,9},{9,10},{10,1... | collective-permute-start | bytes 196616 | tf_op jit(solution)/shard_map/ppermute | solution.py:21
  282.2 1.9 collective-permute-start.1
  284.1 0.9 constant_dynamic-update-slice_fusion
  285.1 4.8 %collective-permute-done.1 = f32[2,4,16,128]{3,2,1,0:T(8,128)S(1)} collective-permute-done((f32[2,4,16,128]{3,2,1,0:T(8,128)S(1)}, f32[2,4,16,128]{3,2,1,0:T(8,128)S(1)}, u32[]{:S(2)}, u32[]{:S(2)}) %collective-permute-start.1) | collective-permute-done | bytes 65568 | tf_op jit(solution)/shard_map/ppermute | solution.py:23
  289.9 1.0 fusion.34
  291.0 1.0 fusion.26
  (19 shorter events, 1.7 us)
Async XLA Ops:
  10.2 43.2 %all-to-all-start = ((s32[128,2,1]{1,2,0:T(1,128)}), s32[128,2,1]{1,2,0:T(1,128)S(1)}, u32[]{:S(2)}, u32[]{:S(2)}) async-start(s32[128,2,1]{1,2,0:T(1,128)} %bitcast.4), calls=%async_computation | async-start | bytes 131072 | tf_op jit(solution)/shard_map/all_to_all | solution.py:94
  53.4 133.2 %all-to-all-start.1 = ((bf16[256,36,512]{2,1,0:T(8,128)(2,1)}), bf16[256,36,512]{2,1,0:T(8,128)(2,1)}, u32[]{:S(2)}, u32[]{:S(2)}) async-start(bf16[256,36,512]{2,1,0:T(8,128)(2,1)} %scatter_fusion), calls=%async_computation.1 | async-start | bytes 20971520 | tf_op jit(solution)/shard_map/all_to_all | solution.py:93
  63.6 211.9 %all-reduce.4.cloned.1.call-start = ((), (), s32[]{:S(2)}) async-start(), calls=%async_computation.2 | async-start | bytes 262144 | tf_op jit(solution)/shard_map/psum | solution.py:114
  276.5 7.7 %collective-permute-start = (f32[2,4,16,128]{3,2,1,0:T(8,128)S(1)}, f32[2,4,16,128]{3,2,1,0:T(8,128)S(1)}, u32[]{:S(2)}, u32[]{:S(2)}) collective-permute-start(f32[2,4,16,128]{3,2,1,0:T(8,128)S(1)} %get-tuple-element.9), channel_id=1, source_target_pairs={{0,1},{1,2},{2,3},{3,4},{4,5},{5,6},{6,7},{7,8},{8,9},{9,10},{10,1... | collective-permute-start | bytes 196616 | tf_op jit(solution)/shard_map/ppermute | solution.py:21
  282.2 7.7 %collective-permute-start.1 = (f32[2,4,16,128]{3,2,1,0:T(8,128)S(1)}, f32[2,4,16,128]{3,2,1,0:T(8,128)S(1)}, u32[]{:S(2)}, u32[]{:S(2)}) collective-permute-start(f32[2,4,16,128]{3,2,1,0:T(8,128)S(1)} %get-tuple-element.10), channel_id=1, source_target_pairs={{1,0},{2,1},{3,2},{4,3},{5,4},{6,5},{7,6},{8,7},{9,8},{10,9},{11,1... | collective-permute-start | bytes 196616 | tf_op jit(solution)/shard_map/ppermute | solution.py:23
Sparse Core Ops, SparseCore 0:
  228.8 46.7 all-reduce.3
where the time goes:
time: 300 us; the launch traced here: 299 us
  waiting for transfers between devices  129 us (43%)
  local copies, waits for them, and re-layouts  81 us (27%)
  other arithmetic  45.6 us (15%)
  starting transfers between devices  28.9 us (10%)
  between operations  13.6 us (5%)
    all_to_all x1, waiting for transfers between devices, local(): lax.all_to_all(outgoing, ('src', 'vol'), split_axis=0, concat_axis=0, til...  77.3 us
    psum x1, waiting for transfers between devices, local(): summed = lax.psum(slab, 'src')  46.9 us
    gather x2, local copies, waits for them, and re-layouts, local(): picked = flat_adjoint[jnp.maximum(arrived_pairs, 0)]  23 us
    scatter x1, local copies, waits for them, and re-layouts, local(): jnp.zeros((slot_total, channels, cells), forward.dtype).at[slot_index]  20.5 us
    sub x1, other arithmetic, correlate(): fwd_split[..., 0, :] * adj_split[..., 0, :]  14 us
    convert_element_type x1, other arithmetic, local(): product = correlate(arrived.astype(jnp.float32), picked.astype(jnp.float32))  12.7 us
    reshape x1, other arithmetic, correlate(): fwd_field.reshape(lead_shape + (NFREQ, 3, 2, fwd_field.shape[-1]))  12.7 us
    all_to_all x1, local copies, waits for them, and re-layouts, local(): lax.all_to_all(outgoing, ('src', 'vol'), split_axis=0, concat_axis=0, til...  10.9 us
  transfers between devices with their start and end apart: 5, of which 3 were waited for; matrix products, arithmetic and copies ran while one was open for 26% of the time, Pallas kernels for 0%

commit v1 on v0

--- a/solution.py
+++ b/solution.py
@@ -111,7 +111,7 @@
         .transpose(2, 3, 0, 4, 1, 5)
         .reshape(2, E, NBY * E, NBZ * E)
     )
-    summed = lax.psum(slab, "src")
+    summed = jnp.sum(jax.lax.all_gather(slab, axis_name="src"), axis=0)
     padded = with_halo(summed, (("vol", 1),), 4)
     field = smooth_axis(padded, 1)
     for axis in (2, 3):

time: 300 us -> 254 us (0.85)
  the two profiles are of different devices: /device:TPU:7 before, /device:TPU:1 now
where the time goes in v1:
time: 254 us; the launch traced here: 253 us
  waiting for transfers between devices  81.7 us (32%)
  local copies, waits for them, and re-layouts  78.6 us (31%)
  other arithmetic  44.8 us (18%)
  starting transfers between devices  34.7 us (14%)
  blocking collectives  12.8 us (5%)
    all_to_all x1, waiting for transfers between devices, local(): lax.all_to_all(outgoing, ('src', 'vol'), split_axis=0, concat_axis=0, til...  78 us
    gather x2, local copies, waits for them, and re-layouts, local(): picked = flat_adjoint[jnp.maximum(arrived_pairs, 0)]  23 us
    scatter x1, local copies, waits for them, and re-layouts, local(): jnp.zeros((slot_total, channels, cells), forward.dtype).at[slot_index]  20.5 us
    sub x1, other arithmetic, correlate(): fwd_split[..., 0, :] * adj_split[..., 0, :]  14 us
    all_gather x1, blocking collectives, local(): summed = jnp.sum(jax.lax.all_gather(slab, axis_name='src'), axis=0)  12.8 us
    convert_element_type x1, other arithmetic, local(): product = correlate(arrived.astype(jnp.float32), picked.astype(jnp.float32))  12.7 us
    reshape x1, other arithmetic, correlate(): fwd_field.reshape(lead_shape + (NFREQ, 3, 2, fwd_field.shape[-1]))  12.7 us
    all_to_all x1, starting transfers between devices, local(): lax.all_to_all(slot_pairs, ('src', 'vol'), split_axis=0, concat_axis=0, t...  11.5 us
  transfers between devices with their start and end apart: 4, of which 2 were waited for; matrix products, arithmetic and copies ran while one was open for 31% of the time, Pallas kernels for 0%

profile of v1, /device:TPU:1, one launch (start us, length us, event | category | flops | bytes accessed | tf_op | source)
XLA Modules:
  0.0 253.3 jit_solution(1560636271729991520)
XLA Ops:
  0.0 0.8 select_reduce_fusion.1
  0.8 0.9 select_reduce_fusion
  1.7 0.2 convert_reduce_fusion
  1.9 1.0 scatter_custom_fusion
  2.9 0.8 all_to_all.11
  3.6 11.5 %all-to-all-start = ((s32[128,2,1]{1,2,0:T(1,128)}), s32[128,2,1]{1,2,0:T(1,128)S(1)}, u32[]{:S(2)}, u32[]{:S(2)}) async-start(s32[128,2,1]{1,2,0:T(1,128)} %bitcast.4), calls=%async_computation | async-start | bytes 131072 | tf_op jit(solution)/shard_map/all_to_all | solution.py:94
  15.1 7.3 %copy.49 = bf16[128,36,512]{2,1,0:T(8,128)(2,1)} copy(bf16[128,36,512]{2,0,1:T(8,128)(2,1)} %param.6) | data formatting | bytes 9437184 | tf_op args[0]
  22.5 4.6 %broadcast_in_dim.33 = bf16[256,36,512]{2,1,0:T(8,128)(2,1)} broadcast(bf16[]{:T(256)} %constant.76.clone.1), dimensions={} | broadcast | bytes 9437186 | tf_op jit(solution)/shard_map/broadcast_in_dim | solution.py:90
  27.0 20.5 %scatter_fusion = bf16[256,36,512]{2,1,0:T(8,128)(2,1)} fusion(bf16[256,36,512]{2,1,0:T(8,128)(2,1)} %broadcast_in_dim.33, s32[128]{0:T(128)S(1)} %fusion.66, bf16[128,36,512]{2,1,0:T(8,128)(2,1)} %copy.49), kind=kCustom, calls=%fused_computation.2 | custom fusion | bytes 14156288 | tf_op jit(solution)/shard_map/scatter | solution.py:90
  47.5 10.3 %all-to-all-start.1 = ((bf16[256,36,512]{2,1,0:T(8,128)(2,1)}), bf16[256,36,512]{2,1,0:T(8,128)(2,1)}, u32[]{:S(2)}, u32[]{:S(2)}) async-start(bf16[256,36,512]{2,1,0:T(8,128)(2,1)} %scatter_fusion), calls=%async_computation.1 | async-start | bytes 20971520 | tf_op jit(solution)/shard_map/all_to_all | solution.py:93
  57.8 2.7 %copy.51 = bf16[4,32,36,512]{3,1,0,2:T(8,128)(2,1)S(1)} copy(bf16[4,32,36,512]{3,1,2,0:T(8,128)(2,1)} %param.11) | data formatting | bytes 9437184 | tf_op args[5]
  60.5 5.1 %copy.52 = bf16[128,36,512]{2,1,0:T(8,128)(2,1)} copy(bf16[128,36,512]{2,0,1:T(8,128)(2,1)S(1)} %bitcast.58) | data formatting | bytes 9437184 | tf_op jit(solution)/shard_map/reshape | solution.py:97
  65.6 0.5 broadcast.393
  66.1 1.0 fusion.69
  67.4 12.1 %gather_fusion = bf16[256,36,512]{2,1,0:T(8,128)(2,1)} fusion(bf16[128,36,512]{2,1,0:T(8,128)(2,1)} %copy.52, s32[1024]{0:T(1024)S(1)} %pad_clamp_fusion), kind=kCustom, calls=%fused_computation | custom fusion | bytes 18875392 | tf_op jit(solution)/shard_map/gather | solution.py:98
  79.5 10.9 %copy.53 = bf16[256,36,512]{2,0,1:T(8,128)(2,1)} copy(bf16[256,36,512]{2,1,0:T(8,128)(2,1)} %gather_fusion) | data formatting | bytes 18874368 | tf_op jit(solution)/shard_map/gather | solution.py:98
  90.4 12.7 %convert.3 = f32[256,6,3,2,512]{4,0,3,2,1:T(8,128)} convert(bf16[256,6,3,2,512]{4,0,3,2,1:T(8,128)(2,1)} %bitcast.56) | non-fusion elementwise | flops 4718592 | bytes 28311552 | tf_op jit(solution)/shard_map/convert_element_type | solution.py:99
  103.2 78.0 %all-to-all-done.1 = bf16[256,36,512]{2,1,0:T(8,128)(2,1)} async-done(((bf16[256,36,512]{2,1,0:T(8,128)(2,1)}), bf16[256,36,512]{2,1,0:T(8,128)(2,1)}, u32[]{:S(2)}, u32[]{:S(2)}) %all-to-all-start.1) | async-done | bytes 9437216 | tf_op jit(solution)/shard_map/all_to_all | solution.py:93
  181.2 10.9 %copy.50 = bf16[256,36,512]{2,0,1:T(8,128)(2,1)} copy(bf16[256,36,512]{2,1,0:T(8,128)(2,1)} %all-to-all-done.1) | data formatting | bytes 18874368 | tf_op jit(solution)/shard_map/all_to_all | solution.py:93
  192.1 12.7 %convert.2 = f32[256,6,3,2,512]{4,0,3,2,1:T(8,128)} convert(bf16[256,6,3,2,512]{4,0,3,2,1:T(8,128)(2,1)} %bitcast.57) | non-fusion elementwise | flops 4718592 | bytes 28311552 | tf_op jit(solution)/shard_map/reshape | solution.py:38
  204.8 14.0 %fusion.1 = f32[256,6,3,512]{3,0,2,1:T(8,128)S(1)} fusion(f32[256,6,3,2,512]{4,0,3,2,1:T(8,128)} %convert.3, f32[256,6,3,2,512]{4,0,3,2,1:T(8,128)} %convert.2), kind=kLoop, calls=%fused_computation.5 | loop fusion | flops 7077888 | bytes 47185920 | tf_op jit(solution)/shard_map/sub | solution.py:41
  218.8 0.4 slice_reduce_fusion.1
  219.2 0.7 slice_reduce_fusion
  220.0 0.3 copy.54
  220.4 0.7 convolution_bitcast_fusion
  221.0 0.6 copy.55
  221.7 1.0 all_gather_reshape.3
  222.7 12.8 %all_gather.3 = f32[4,2,8,16,128]{4,3,2,1,0:T(8,128)S(1)} all-gather(f32[1,2,8,16,128]{4,3,2,1,0:T(8,128)S(1)} %all_gather_reshape.3), channel_id=1, replica_groups=mesh['src'=4,'vol'=32] {'src'}, dimensions={0}, use_global_device_ids=true | all-gather | bytes 655360 | tf_op jit(solution)/shard_map/all_gather | solution.py:114
  235.5 11.0 %collective-permute-start = (f32[2,4,16,128]{3,2,1,0:T(8,128)S(1)}, f32[2,4,16,128]{3,2,1,0:T(8,128)S(1)}, u32[]{:S(2)}, u32[]{:S(2)}) collective-permute-start(f32[2,4,16,128]{3,2,1,0:T(8,128)S(1)} %get-tuple-element.7), channel_id=1, source_target_pairs={{0,1},{1,2},{2,3},{3,4},{4,5},{5,6},{6,7},{7,8},{8,9},{9,10},{10,1... | collective-permute-start | bytes 196616 | tf_op jit(solution)/shard_map/ppermute | solution.py:21
  246.5 1.9 collective-permute-start.1
  248.5 3.6 %collective-permute-done.1 = f32[2,4,16,128]{3,2,1,0:T(8,128)S(1)} collective-permute-done((f32[2,4,16,128]{3,2,1,0:T(8,128)S(1)}, f32[2,4,16,128]{3,2,1,0:T(8,128)S(1)}, u32[]{:S(2)}, u32[]{:S(2)}) %collective-permute-start.1) | collective-permute-done | bytes 65568 | tf_op jit(solution)/shard_map/ppermute | solution.py:23
  252.3 1.0 fusion.46
  (15 shorter events, 0.7 us)
Async XLA Ops:
  3.6 43.9 %all-to-all-start = ((s32[128,2,1]{1,2,0:T(1,128)}), s32[128,2,1]{1,2,0:T(1,128)S(1)}, u32[]{:S(2)}, u32[]{:S(2)}) async-start(s32[128,2,1]{1,2,0:T(1,128)} %bitcast.4), calls=%async_computation | async-start | bytes 131072 | tf_op jit(solution)/shard_map/all_to_all | solution.py:94
  47.5 133.7 %all-to-all-start.1 = ((bf16[256,36,512]{2,1,0:T(8,128)(2,1)}), bf16[256,36,512]{2,1,0:T(8,128)(2,1)}, u32[]{:S(2)}, u32[]{:S(2)}) async-start(bf16[256,36,512]{2,1,0:T(8,128)(2,1)} %scatter_fusion), calls=%async_computation.1 | async-start | bytes 20971520 | tf_op jit(solution)/shard_map/all_to_all | solution.py:93
  235.5 12.9 %collective-permute-start = (f32[2,4,16,128]{3,2,1,0:T(8,128)S(1)}, f32[2,4,16,128]{3,2,1,0:T(8,128)S(1)}, u32[]{:S(2)}, u32[]{:S(2)}) collective-permute-start(f32[2,4,16,128]{3,2,1,0:T(8,128)S(1)} %get-tuple-element.7), channel_id=1, source_target_pairs={{0,1},{1,2},{2,3},{3,4},{4,5},{5,6},{6,7},{7,8},{8,9},{9,10},{10,1... | collective-permute-start | bytes 196616 | tf_op jit(solution)/shard_map/ppermute | solution.py:21
  246.5 5.6 %collective-permute-start.1 = (f32[2,4,16,128]{3,2,1,0:T(8,128)S(1)}, f32[2,4,16,128]{3,2,1,0:T(8,128)S(1)}, u32[]{:S(2)}, u32[]{:S(2)}) collective-permute-start(f32[2,4,16,128]{3,2,1,0:T(8,128)S(1)} %get-tuple-element.8), channel_id=1, source_target_pairs={{1,0},{2,1},{3,2},{4,3},{5,4},{6,5},{7,6},{8,7},{9,8},{10,9},{11,1... | collective-permute-start | bytes 196616 | tf_op jit(solution)/shard_map/ppermute | solution.py:23
